TPU v7x, 128 devices: a whole 4x4x4 slice. The times are simulated.
128 devices in a mesh: layer: 16 (over y, x), prow: 4 (over z), pcol: 2 (over core).
Axes of the slice: x: 4, y: 4, z: 4, core: 2. Of those that a mesh axis runs over, the one named last changes fastest.
Arguments:
- front: bfloat16 [16, 2048, 32768], P('layer', 'prow', 'pcol'), may hold values from -6 to 6
- pivots: bfloat16 [16, 2, 256, 32768], P('layer', None, 'prow', 'pcol'), may hold values from -0.8984375 to 0.8984375
- inverses: bfloat16 [16, 2, 256, 256], P('layer'), may hold values from -0.1875 to 0.1875
- slab_pattern: int32 [16, 8, 128], P('layer', 'prow', 'pcol'), may hold values 0 or 1
- pivot_pattern: int32 [16, 2, 128], P('layer', None, 'pcol'), may hold values from 0 to 1, as said below
Outputs:
- ancestor: float32 [4, 16, 32, 32768], P('prow', 'layer', None, 'pcol')
- lower: bfloat16 [16, 2048, 512], P('layer', 'prow')
- upper: bfloat16 [16, 256, 32768], P('layer', 'prow', 'pcol')
Inputs may be any that keep to these rules, and one draw needn't show every extreme that they name: `pivot_pattern`: each entry says whether that block of the pivot rows is structurally nonzero. `slab_pattern`: each entry says whether that block of the front rows is structurally nonzero.
All inputs are finite; a program needn't handle non-finite values.
Results may differ from a plain program's by a relative error of at most 0.014.
Values may be sent and summed in bfloat16 or wider, within the bound.
No kernel may reach another device: no remote copies, remote signals or barrier semaphores. Data moves between devices by JAX's collectives and lax.ppermute only.
A program may use at most 192 MiB of HBM per device.

v0:
```python
import jax
import jax.numpy as jnp
from jax import lax
from jax.sharding import PartitionSpec as P


def spread(value, axis, root):
    mine = lax.axis_index(axis) == root
    return lax.psum(jnp.where(mine, value, jnp.zeros_like(value)), axis)


def on_device(front, pivots, inverses, slab_pattern, pivot_pattern):
    block_size = inverses.shape[-1]
    panel_width = 2 * block_size
    row_count = front.shape[1]
    col_count = front.shape[2]
    own_rows = pivots.shape[2]
    masked = (
        front[0].reshape(row_count // block_size, block_size, col_count // block_size, block_size)
        * slab_pattern[0].astype(jnp.bfloat16)[:, None, :, None]
    ).reshape(row_count, col_count)
    pivot_masked = (
        pivots[0].reshape(2, own_rows, col_count // block_size, block_size)
        * pivot_pattern[0].astype(jnp.bfloat16)[:, None, :, None]
    ).reshape(2, own_rows, col_count)
    first_inverse = inverses[0, 0]
    second_inverse = inverses[0, 1]
    row_offset = lax.axis_index("prow") * own_rows
    gathered = lax.all_gather(pivot_masked, "prow", axis=1, tiled=True)
    panel_cols = spread(
        jnp.concatenate(
            [masked[:, :panel_width], gathered[0][:, :panel_width], gathered[1][:, :panel_width]], 0
        ),
        "pcol",
        0,
    )
    front_cols = panel_cols[:row_count]
    pivot_cols = panel_cols[row_count : row_count + block_size]
    second_cols = panel_cols[row_count + block_size :]
    lower_pivot = jnp.dot(
        second_cols[:, :block_size], first_inverse, preferred_element_type=jnp.float32
    ).astype(jnp.bfloat16)
    upper_first = gathered[0]
    upper_second = (
        gathered[1].astype(jnp.float32)
        - jnp.dot(lower_pivot, upper_first, preferred_element_type=jnp.float32)
    ).astype(jnp.bfloat16)
    upper_own = lax.dynamic_slice_in_dim(upper_second, row_offset, own_rows, 0)
    lower_first = jnp.dot(
        front_cols[:, :block_size], first_inverse, preferred_element_type=jnp.float32
    ).astype(jnp.bfloat16)
    carried = (
        front_cols[:, block_size:].astype(jnp.float32)
        - jnp.dot(
            lower_first, pivot_cols[:, block_size:panel_width], preferred_element_type=jnp.float32
        )
    ).astype(jnp.bfloat16)
    lower_second = jnp.dot(carried, second_inverse, preferred_element_type=jnp.float32).astype(
        jnp.bfloat16
    )
    lower_panel = jnp.concatenate([lower_first, lower_second], 1)
    stacked = jnp.concatenate([upper_first, upper_second], 0)
    col_index = lax.axis_index("pcol") * col_count + jnp.arange(col_count, dtype=jnp.int32)
    retained = col_index >= panel_width
    schur_rows = masked.astype(jnp.float32) - jnp.dot(
        lower_panel, stacked, preferred_element_type=jnp.float32
    )
    schur_rows = jnp.where(retained[None, :], schur_rows, jnp.zeros_like(schur_rows))
    summed = lax.psum_scatter(
        schur_rows.astype(jnp.bfloat16), "layer", scatter_dimension=0, tiled=True
    ).astype(jnp.float32)
    ancestor = summed.reshape(1, 1, summed.shape[0], col_count)
    return (ancestor, lower_panel[None], upper_own[None])


def solution(mesh):
    placed = (
        P("layer", "prow", "pcol"),
        P("layer", None, "prow", "pcol"),
        P("layer", None, None, None),
        P("layer", "prow", "pcol"),
        P("layer", None, "pcol"),
    )
    return jax.shard_map(
        on_device,
        mesh=mesh,
        in_specs=placed,
        out_specs=(
            P("prow", "layer", None, "pcol"),
            P("layer", "prow", None),
            P("layer", "prow", "pcol"),
        ),
        check_vma=False,
    )
```

profile of v0, /device:TPU:1, one launch (start us, length us, event | category | flops | bytes accessed | tf_op | source)
XLA Modules:
  0.0 362.8 jit_solution(13036660158709411677)
XLA Ops:
  7.2 0.0 all-gather.2.cloned.1.call-start
  7.2 0.7 convert_bitcast_fusion
  7.9 0.1 broadcast_bitcast_fusion
  8.0 0.1 copy.10
  8.1 4.8 %bitcast_multiply_fusion.1 = bf16[2,64,16384]{2,1,0:T(8,128)(2,1)} fusion(bf16[1,2,64,16384]{3,2,1,0:T(8,128)(2,1)} %param.6, bf16[2,16384]{1,0:T(2,128)(2,1)S(1)} %bitcast.40), kind=kLoop, calls=%fused_computation.9 | loop fusion | flops 2097152 | bytes 8454144 | tf_op jit(solution)/shard_map/mul | solution.py:23
  12.8 0.0 all-gather.2.cloned.1.call-update
  12.9 0.0 all-reduce.2.cloned.1.call-start
  12.9 0.7 convert_bitcast_fusion.1
  13.6 2.7 mul.31
  16.3 10.4 %copy.9 = bf16[64,8,64,256]{3,1,2,0:T(8,128)(2,1)S(1)} copy(bf16[64,8,64,256]{3,2,1,0:T(8,128)(2,1)S(1)} %bitcast.39) | data formatting | bytes 33554432
  26.8 9.7 %bitcast_multiply_fusion = bf16[512,16384]{1,0:T(8,128)(2,1)S(1)} fusion(bf16[512,16384]{1,0:T(8,128)(2,1)S(1)} %bitcast.38, bf16[1,512,16384]{2,1,0:T(8,128)(2,1)} %param.5), kind=kLoop, calls=%fused_computation.6 | loop fusion | flops 8388608 | bytes 50331648 | tf_op jit(solution)/shard_map/mul | solution.py:19
  36.5 0.0 copy-start
  36.5 5.9 %copy-done = bf16[512,16384]{1,0:T(8,128)(2,1)} copy-done((bf16[512,16384]{1,0:T(8,128)(2,1)}, bf16[512,16384]{1,0:T(8,128)(2,1)S(1)}, u32[]{:S(2)}) %copy-start) | copy-done | bytes 16777240
  42.5 0.0 copy-start.2
  42.5 127.9 %all-gather.2.cloned.1.call-done = bf16[2,256,16384]{2,1,0:T(8,128)(2,1)} async-done(((bf16[2,64,16384]{2,1,0:T(8,128)(2,1)}), bf16[2,256,16384]{2,1,0:T(8,128)(2,1)}) %all-gather.2.cloned.1.call-update) | async-done | bytes 16777232 | tf_op jit(solution)/shard_map/all_gather | solution.py:29
  170.4 6.7 %slice_bitcast_fusion.1 = (bf16[256,16384]{1,0:T(8,128)(2,1)S(1)}, bf16[256,16384]{1,0:T(8,128)(2,1)S(1)}) fusion(bf16[2,256,16384]{2,1,0:T(8,128)(2,1)} %all-gather.2.cloned.1.call-done), kind=kLoop, calls=%fused_computation.8 | loop fusion | bytes 33554432 | tf_op jit(solution)/shard_map/squeeze | solution.py:32
  177.1 0.0 copy-start.1
  177.2 3.2 copy-done.1
  180.4 1.2 maximum_select_fusion
  181.6 0.0 all-reduce.2.cloned.1.call-update
  181.6 0.0 reduce-scatter.2.cloned.1.call-start
  181.7 26.6 %all-reduce.2.cloned.1.call-done = bf16[1024,512]{1,0:T(8,128)(2,1)} async-done(((bf16[1024,512]{1,0:T(8,128)(2,1)}), bf16[1024,512]{1,0:T(8,128)(2,1)}) %all-reduce.2.cloned.1.call-update) | async-done | bytes 1048592 | tf_op jit(solution)/shard_map/psum | solution.py:9
  208.3 0.0 copy-done.2
  208.3 9.3 %fusion = bf16[256,16384]{1,0:T(8,128)(2,1)} fusion(bf16[1024,512]{1,0:T(8,128)(2,1)} %all-reduce.2.cloned.1.call-done, bf16[1,2,256,256]{3,2,1,0:T(8,128)(2,1)S(1)} %copy-done.2, bf16[2,256,16384]{2,1,0:T(8,128)(2,1)} %all-gather.2.cloned.1.call-done), kind=kOutput, calls=%fused_computation.2 | convolution fusion | flops 2193686528 | bytes 25427968 | tf_op jit(solution)/shard_map/dot_general | solution.py:46
  217.6 1.2 convolution_convert_fusion.1
  218.8 1.5 convolution_convert_fusion
  220.3 22.0 %select_convert_fusion = bf16[512,16384]{1,0:T(8,128)(2,1)} fusion(bf16[512,16384]{1,0:T(8,128)(2,1)} %copy-done, bf16[256,16384]{1,0:T(8,128)(2,1)} %fusion, bf16[256,16384]{1,0:T(8,128)(2,1)} %copy-done.1, pred[16384]{0:T(1024)(128)(4,1)S(1)} %add_compare_fusion, bf16[512,256]{0,1:T(8,128)(2,1)S(1)} %convolution_convert_fusion, ...), kind=kOutput, calls=%fused_computation | convolution fusion | flops 8658092032 | bytes 50872320 | tf_op jit(solution)/shard_map/dot_general | solution.py:65
  242.2 0.0 reduce-scatter.2.cloned.1.call-update
  242.3 1.0 copy.8
  243.3 3.0 dynamic-slice_bitcast_fusion
  246.4 107.2 %reduce-scatter.2.cloned.1.call-done = bf16[32,16384]{1,0:T(8,128)(2,1)} async-done(((bf16[512,16384]{1,0:T(8,128)(2,1)}), bf16[32,16384]{1,0:T(8,128)(2,1)}) %reduce-scatter.2.cloned.1.call-update) | async-done | bytes 1048592 | tf_op jit(solution)/shard_map/reduce_scatter | solution.py:69
  353.6 2.7 bitcast_convert_fusion
  (5 shorter events, 0.1 us)
Async XLA Ops:
  7.2 163.2 %all-gather.2.cloned.1.call-start = ((), (), s32[]{:S(2)}) async-start(), calls=%async_computation.1 | async-start | bytes 20971520 | tf_op jit(solution)/shard_map/all_gather | solution.py:29
  12.9 195.4 %all-reduce.2.cloned.1.call-start = ((), (), s32[]{:S(2)}) async-start(), calls=%async_computation.2 | async-start | bytes 2097152 | tf_op jit(solution)/shard_map/psum | solution.py:9
  36.5 6.0 %copy-start = (bf16[512,16384]{1,0:T(8,128)(2,1)}, bf16[512,16384]{1,0:T(8,128)(2,1)S(1)}, u32[]{:S(2)}) copy-start(bf16[512,16384]{1,0:T(8,128)(2,1)S(1)} %bitcast_multiply_fusion) | copy-start | bytes 50331652
  42.5 165.8 %copy-start.2 = (bf16[1,2,256,256]{3,2,1,0:T(8,128)(2,1)S(1)}, bf16[1,2,256,256]{3,2,1,0:T(8,128)(2,1)}, u32[]{:S(2)}) copy-start(bf16[1,2,256,256]{3,2,1,0:T(8,128)(2,1)} %param.7) | copy-start | bytes 786436
  177.1 3.2 copy-start.1
  181.6 172.0 %reduce-scatter.2.cloned.1.call-start = ((), (), s32[]{:S(2)}) async-start(), calls=%async_computation.3 | async-start | bytes 17825792 | tf_op jit(solution)/shard_map/reduce_scatter | solution.py:69
Sparse Core Ops, SparseCore 0:
  13.0 157.3 all-gather.1
  181.7 26.5 all-reduce.1
  242.4 111.1 reduce-scatter.1
where the time goes:
time: 363 us
  waiting for transfers between devices  262 us (72%)
  matrix products  33.9 us (9%)
  local copies, waits for them, and re-layouts  33.3 us (9%)
  other arithmetic  19.8 us (5%)
  between operations  13.9 us (4%)
    all_gather x1, waiting for transfers between devices, on_device(): gathered = lax.all_gather(pivot_masked, 'prow', axis=1, tiled=True)  128 us
    reduce_scatter x1, waiting for transfers between devices, on_device(): lax.psum_scatter(schur_rows.astype(jnp.bfloat16), 'layer', scatter_dimens...  107 us
    psum x1, waiting for transfers between devices, spread(): return lax.psum(jnp.where(mine, value, jnp.zeros_like(value)), axis)  26.6 us
    dot_general x1, matrix products, on_device(): jnp.dot(lower_panel, stacked, preferred_element_type=jnp.float32)  22 us
    unnamed x10, local copies, waits for them, and re-layouts  20.7 us
    mul x1, other arithmetic, on_device(): front[0]  9.72 us
    dot_general x1, matrix products, on_device(): jnp.dot(lower_pivot, upper_first, preferred_element_type=jnp.float32)  9.25 us
  transfers between devices with their start and end apart: 3, of which 3 were waited for; matrix products, arithmetic and copies ran while one was open for 8% of the time, Pallas kernels for 0%

commit v1 on v0

--- a/solution.py
+++ b/solution.py
@@ -2,6 +2,11 @@
 import jax.numpy as jnp
 from jax import lax
 from jax.sharding import PartitionSpec as P
+
+
+def tiled_gather(x, axis, dim):
+    copies = jnp.concatenate([x] * lax.axis_size(axis), axis=dim)
+    return lax.all_to_all(copies, axis, dim, dim, tiled=True)
 
 
 def spread(value, axis, root):
@@ -26,7 +31,7 @@
     first_inverse = inverses[0, 0]
     second_inverse = inverses[0, 1]
     row_offset = lax.axis_index("prow") * own_rows
-    gathered = lax.all_gather(pivot_masked, "prow", axis=1, tiled=True)
+    gathered = tiled_gather(pivot_masked, "prow", 1)
     panel_cols = spread(
         jnp.concatenate(
             [masked[:, :panel_width], gathered[0][:, :panel_width], gathered[1][:, :panel_width]], 0

time: 363 us -> 475 us (1.31)
  local copies, waits for them, and re-layouts: 33.3 us -> 81.5 us
  waiting for transfers between devices: 262 us -> 290 us
  other arithmetic: 19.8 us -> 47.5 us
  starting transfers between devices: 0.12 us -> 7.59 us
    all_to_all x0 -> x1, waiting for transfers between devices: none -> 157 us  [tiled_gather(): return lax.all_to_all(copies, axis, dim, dim, tiled=True)]
    all_gather x1 -> x0, waiting for transfers between devices: 128 us -> none  [on_device(): gathered = lax.all_gather(pivot_masked, 'prow', axis=1, tiled=True)]
    slice x1 -> x2, local copies, waits for them, and re-layouts: 0.02 us -> 33.4 us  [on_device(): gathered[1][:, :panel_width]]
    concatenate x0 -> x1, other arithmetic: none -> 25.9 us  [tiled_gather(): copies = jnp.concatenate([x] * lax.axis_size(axis), axis=dim)]
    squeeze x1, local copies, waits for them, and re-layouts: 6.73 us -> 24 us  [on_device(): gathered[1][:, :panel_width]]
    all_to_all x0 -> x1, starting transfers between devices: none -> 7.1 us  [tiled_gather(): return lax.all_to_all(copies, axis, dim, dim, tiled=True)]
  transfers between devices with their start and end apart: 3 -> 3, of which waited for: 3 -> 3; matrix products, arithmetic and copies ran while one was open for 8% -> 5% of each run, Pallas kernels for 0% -> 0%
where the time goes in v1:
time: 475 us
  waiting for transfers between devices  290 us (61%)
  local copies, waits for them, and re-layouts  81.5 us (17%)
  other arithmetic  47.5 us (10%)
  matrix products  33.9 us (7%)
  between operations  14.2 us (3%)
  starting transfers between devices  7.59 us (2%)
    all_to_all x1, waiting for transfers between devices, tiled_gather(): return lax.all_to_all(copies, axis, dim, dim, tiled=True)  157 us
    reduce_scatter x1, waiting for transfers between devices, on_device(): lax.psum_scatter(schur_rows.astype(jnp.bfloat16), 'layer', scatter_dimens...  107 us
    slice x2, local copies, waits for them, and re-layouts, on_device(): gathered[1][:, :panel_width]  33.4 us
    concatenate x1, other arithmetic, tiled_gather(): copies = jnp.concatenate([x] * lax.axis_size(axis), axis=dim)  25.9 us
    psum x1, waiting for transfers between devices, spread(): return lax.psum(jnp.where(mine, value, jnp.zeros_like(value)), axis)  25.3 us
    squeeze x1, local copies, waits for them, and re-layouts, on_device(): gathered[1][:, :panel_width]  24 us
    dot_general x1, matrix products, on_device(): jnp.dot(lower_panel, stacked, preferred_element_type=jnp.float32)  22 us
    unnamed x10, local copies, waits for them, and re-layouts  17.3 us
  transfers between devices with their start and end apart: 3, of which 3 were waited for; matrix products, arithmetic and copies ran while one was open for 5% of the time, Pallas kernels for 0%

profile of v1, /device:TPU:1, one launch (start us, length us, event | category | flops | bytes accessed | tf_op | source)
XLA Modules:
  0.0 474.6 jit_solution(18373995428966968753)
XLA Ops:
  7.2 0.7 convert_bitcast_fusion
  7.8 0.1 broadcast_bitcast_fusion
  7.9 0.1 copy.16
  8.0 8.7 %bitcast_multiply_fusion.1 = bf16[2,64,16384]{2,0,1:T(2,128)(2,1)S(1)} fusion(bf16[1,2,64,16384]{3,2,1,0:T(8,128)(2,1)} %param.6, bf16[2,16384]{1,0:T(2,128)(2,1)S(1)} %bitcast.38), kind=kLoop, calls=%fused_computation.10 | loop fusion | flops 2097152 | bytes 8454144 | tf_op jit(solution)/shard_map/mul | solution.py:28
  16.7 25.9 %pad_maximum_fusion = bf16[2,256,16384]{2,0,1:T(2,128)(2,1)} fusion(bf16[2,64,16384]{2,0,1:T(2,128)(2,1)S(1)} %bitcast_multiply_fusion.1), kind=kLoop, calls=%fused_computation.3 | loop fusion | flops 25165824 | bytes 20971520 | tf_op jit(solution)/shard_map/concatenate | solution.py:8
  42.7 0.0 copy-start.2
  42.7 7.1 %all-to-all-start = ((bf16[2,256,16384]{2,0,1:T(2,128)(2,1)}), bf16[2,256,16384]{2,0,1:T(2,128)(2,1)}, u32[]{:S(2)}, u32[]{:S(2)}) async-start(bf16[2,256,16384]{2,0,1:T(2,128)(2,1)} %pad_maximum_fusion), calls=%async_computation | async-start | bytes 33554432 | tf_op jit(solution)/shard_map/all_to_all | solution.py:9
  49.8 0.2 all-reduce.2.cloned.1.call-start
  50.0 0.0 copy-done.2
  50.0 2.7 mul.31
  52.8 10.4 %copy.15 = bf16[64,8,64,256]{3,1,2,0:T(8,128)(2,1)S(1)} copy(bf16[64,8,64,256]{3,2,1,0:T(8,128)(2,1)S(1)} %bitcast.37) | data formatting | bytes 33554432
  63.2 8.3 %bitcast_multiply_fusion = bf16[512,16384]{1,0:T(8,128)(2,1)S(1)} fusion(bf16[512,16384]{1,0:T(8,128)(2,1)S(1)} %bitcast.36, bf16[1,512,16384]{2,1,0:T(8,128)(2,1)} %param.5), kind=kLoop, calls=%fused_computation.7 | loop fusion | flops 8388608 | bytes 50331648 | tf_op jit(solution)/shard_map/mul | solution.py:24
  71.5 0.0 copy-start
  71.5 5.7 %copy-done = bf16[512,16384]{1,0:T(8,128)(2,1)} copy-done((bf16[512,16384]{1,0:T(8,128)(2,1)}, bf16[512,16384]{1,0:T(8,128)(2,1)S(1)}, u32[]{:S(2)}) %copy-start) | copy-done | bytes 16777240
  77.3 157.4 %all-to-all-done = bf16[2,256,16384]{2,0,1:T(2,128)(2,1)} async-done(((bf16[2,256,16384]{2,0,1:T(2,128)(2,1)}), bf16[2,256,16384]{2,0,1:T(2,128)(2,1)}, u32[]{:S(2)}, u32[]{:S(2)}) %all-to-all-start) | async-done | bytes 16777248 | tf_op jit(solution)/shard_map/all_to_all | solution.py:9
  234.7 32.5 %fusion.22 = (bf16[1,256,16384]{2,0,1:T(2,128)(2,1)S(1)}, bf16[1,256,16384]{2,0,1:T(2,128)(2,1)}) fusion(bf16[2,256,16384]{2,0,1:T(2,128)(2,1)} %all-to-all-done), kind=kLoop, calls=%fused_computation.37 | loop fusion | bytes 33554432 | tf_op jit(solution)/shard_map/slice | solution.py:37
  267.2 0.0 copy-start.1
  267.2 24.0 %copy_bitcast_fusion = (bf16[256,16384]{1,0:T(8,128)(2,1)}, bf16[256,16384]{1,0:T(8,128)(2,1)}) fusion(bf16[1,256,16384]{2,0,1:T(2,128)(2,1)S(1)} %get-tuple-element.9, bf16[1,256,16384]{2,0,1:T(2,128)(2,1)} %get-tuple-element.10), kind=kLoop, calls=%fused_computation.8 | loop fusion | bytes 33554432 | tf_op jit(solution)/shard_map/squeeze | solution.py:37
  291.2 1.0 slice.55
  292.2 1.0 slice.57
  293.1 1.2 maximum_select_fusion
  294.3 0.0 all-reduce.2.cloned.1.call-update
  294.3 0.3 reduce-scatter.2.cloned.1.call-start
  294.6 25.3 %all-reduce.2.cloned.1.call-done = bf16[1024,512]{1,0:T(8,128)(2,1)} async-done(((bf16[1024,512]{1,0:T(8,128)(2,1)}), bf16[1024,512]{1,0:T(8,128)(2,1)}) %all-reduce.2.cloned.1.call-update) | async-done | bytes 1048592 | tf_op jit(solution)/shard_map/psum | solution.py:14
  320.0 0.0 copy-done.1
  320.0 1.2 convolution_convert_fusion.1
  321.2 9.2 %fusion = bf16[256,16384]{1,0:T(8,128)(2,1)} fusion(bf16[256,16384]{1,0:T(8,128)(2,1)} %get-tuple-element.12, bf16[256,16384]{1,0:T(8,128)(2,1)} %get-tuple-element.11, bf16[1024,512]{1,0:T(8,128)(2,1)} %all-reduce.2.cloned.1.call-done, bf16[1,2,256,256]{3,2,1,0:T(8,128)(2,1)S(1)} %copy-done.1), kind=kOutput, calls=%fused_computation.2 | convolution fusion | flops 2193686528 | bytes 25427968 | tf_op jit(solution)/shard_map/dot_general | solution.py:51
  330.4 1.5 convolution_convert_fusion
  331.9 22.0 %select_convert_fusion = bf16[512,16384]{1,0:T(8,128)(2,1)} fusion(bf16[512,16384]{1,0:T(8,128)(2,1)} %copy-done, bf16[256,16384]{1,0:T(8,128)(2,1)} %fusion, bf16[256,16384]{1,0:T(8,128)(2,1)} %get-tuple-element.12, pred[16384]{0:T(1024)(128)(4,1)S(1)} %add_compare_fusion, bf16[512,256]{0,1:T(8,128)(2,1)S(1)} %convolution_convert_fusion, ...), kind=kOutput, calls=%fused_computation | convolution fusion | flops 8658092032 | bytes 50872320 | tf_op jit(solution)/shard_map/dot_general | solution.py:70
  353.9 0.0 reduce-scatter.2.cloned.1.call-update
  353.9 1.0 copy.12
  354.9 3.0 dynamic-slice_bitcast_fusion
  358.0 107.1 %reduce-scatter.2.cloned.1.call-done = bf16[32,16384]{1,0:T(8,128)(2,1)} async-done(((bf16[512,16384]{1,0:T(8,128)(2,1)}), bf16[32,16384]{1,0:T(8,128)(2,1)}) %reduce-scatter.2.cloned.1.call-update) | async-done | bytes 1048592 | tf_op jit(solution)/shard_map/reduce_scatter | solution.py:74
  465.1 2.7 bitcast_convert_fusion
  (4 shorter events, 0.1 us)
Async XLA Ops:
  42.7 7.3 %copy-start.2 = (s32[1,2,64]{2,1,0:T(2,128)S(1)}, s32[1,2,64]{2,1,0:T(2,128)}, u32[]{:S(2)}) copy-start(s32[1,2,64]{2,1,0:T(2,128)} %param.8) | copy-start | bytes 1540
  42.7 192.1 %all-to-all-start = ((bf16[2,256,16384]{2,0,1:T(2,128)(2,1)}), bf16[2,256,16384]{2,0,1:T(2,128)(2,1)}, u32[]{:S(2)}, u32[]{:S(2)}) async-start(bf16[2,256,16384]{2,0,1:T(2,128)(2,1)} %pad_maximum_fusion), calls=%async_computation | async-start | bytes 33554432 | tf_op jit(solution)/shard_map/all_to_all | solution.py:9
  49.8 270.2 %all-reduce.2.cloned.1.call-start = ((), (), s32[]{:S(2)}) async-start(), calls=%async_computation.2 | async-start | bytes 2097152 | tf_op jit(solution)/shard_map/psum | solution.py:14
  71.5 5.7 %copy-start = (bf16[512,16384]{1,0:T(8,128)(2,1)}, bf16[512,16384]{1,0:T(8,128)(2,1)S(1)}, u32[]{:S(2)}) copy-start(bf16[512,16384]{1,0:T(8,128)(2,1)S(1)} %bitcast_multiply_fusion) | copy-start | bytes 50331652
  267.2 52.8 %copy-start.1 = (bf16[1,2,256,256]{3,2,1,0:T(8,128)(2,1)S(1)}, bf16[1,2,256,256]{3,2,1,0:T(8,128)(2,1)}, u32[]{:S(2)}) copy-start(bf16[1,2,256,256]{3,2,1,0:T(8,128)(2,1)} %param.7) | copy-start | bytes 786436
  294.3 170.7 %reduce-scatter.2.cloned.1.call-start = ((), (), s32[]{:S(2)}) async-start(), calls=%async_computation.3 | async-start | bytes 17825792 | tf_op jit(solution)/shard_map/reduce_scatter | solution.py:74
Sparse Core Ops, SparseCore 0:
  294.5 25.4 all-reduce.1
  354.0 111.0 reduce-scatter.1
